TPU v7x, 128 devices: a whole 4x4x4 slice. The times are simulated.
128 devices in a mesh: section: 2 (over core), seq: 4 (over x), tensor: 16 (over z, y).
Axes of the slice: x: 4, y: 4, z: 4, core: 2. Of those that a mesh axis runs over, the one named last changes fastest.
Arguments:
- queries: bfloat16 [2560, 8192], P(('section', 'seq'), 'tensor'), may hold values from -200 to 200
- neighbours: bfloat16 [10240, 8192], P(('section', 'seq', 'tensor')), may hold values from -6 to 6
- kv_weight: bfloat16 [2, 8192, 8192], P(None, None, 'tensor'), may hold values from -0.0625 to 0.0625
- out_weight: bfloat16 [8192, 8192], P('tensor'), may hold values from -0.5 to 0.5
- slot_map: int32 [40], replicated, may hold values from 0 to 39, as said below
Outputs:
- mixed: bfloat16 [2560, 8192], P(('section', 'seq', 'tensor'))
Inputs may be any that keep to these rules, and one draw needn't show every extreme that they name: `slot_map`: distinct numbers; slot s lies on encoder shard s // 5; at most 2 spans of one sequence shard map to one encoder shard, and that many do for some pair of shards.
All inputs are finite; a program needn't handle non-finite values.
Results may differ from a plain program's by a relative error of at most 0.013.
Values may be sent and summed in bfloat16 or wider, within the bound.
No kernel may reach another device: no remote copies, remote signals or barrier semaphores. Data moves between devices by JAX's collectives and lax.ppermute only.
A program may use at most 128 MiB of HBM per device.

v0:
```python
import math
import jax
import jax.numpy as jnp
from jax import lax
from jax.sharding import PartitionSpec as P

HD = 128
SPAN = 64
PEER = 2
CH_DEV = 5
CAPC = 5
KEYS = 256


def attend(query_block, keys, values):
    scores = jnp.einsum("bqhd,bkhd->bhqk", query_block, keys, preferred_element_type=jnp.float32)
    scores = scores * (1.0 / math.sqrt(HD))
    peak = jnp.max(scores, axis=-1, keepdims=True)
    expo = jnp.exp(scores - peak)
    weights = (expo / jnp.sum(expo, axis=-1, keepdims=True)).astype(jnp.bfloat16)
    result = jnp.einsum("bhqk,bkhd->bqhd", weights, values, preferred_element_type=jnp.float32)
    return result.astype(jnp.bfloat16)


def on_device(queries, neighbours, kv_weight, out_weight, slot_map):
    groups = lax.axis_size(("section", "seq"))
    group_index = lax.axis_index(("section", "seq"))
    tensor_size = lax.axis_size("tensor")
    cols = kv_weight.shape[2]
    heads_local = cols // HD
    spans = slot_map.shape[0]
    rows_local = neighbours.shape[0]
    span_ids = jnp.arange(spans, dtype=jnp.int32)
    owner_shard = slot_map // CAPC
    slot_index = slot_map % CAPC
    seq_owner = span_ids // CH_DEV
    earlier = (seq_owner[:, None] == seq_owner[None, :]) & (
        owner_shard[:, None] == owner_shard[None, :]
    )
    earlier = earlier & (span_ids[None, :] < span_ids[:, None])
    arrival = jnp.sum(earlier.astype(jnp.int32), axis=1)
    peer_ids = jnp.arange(groups, dtype=jnp.int32)[:, None, None]
    place_ids = jnp.arange(PEER, dtype=jnp.int32)[None, :, None]
    own_spans = group_index * CH_DEV + jnp.arange(CH_DEV, dtype=jnp.int32)
    own_owner = owner_shard[own_spans]
    own_arrival = arrival[own_spans]
    pick_q = (own_owner[None, None, :] == peer_ids) & (own_arrival[None, None, :] == place_ids)
    send_q_idx = jnp.sum(
        jnp.where(pick_q, jnp.arange(CH_DEV, dtype=jnp.int32)[None, None, :], 0), axis=-1
    )
    query_blocks = queries.reshape(CH_DEV, SPAN, cols)
    send_q = query_blocks[send_q_idx]
    q_by_shift = [send_q[group_index]]
    for k in range(1, groups):
        block = lax.dynamic_index_in_dim(send_q, (group_index + k) % groups, 0, keepdims=False)
        pairs = [(s, (s + k) % groups) for s in range(groups)]
        q_by_shift.append(lax.ppermute(block, ("section", "seq"), pairs))
    recv_q = jnp.stack(q_by_shift)
    my_slots = group_index * CAPC + jnp.arange(CAPC, dtype=jnp.int32)
    hit = slot_map[None, :] == my_slots[:, None]
    slot_span = jnp.sum(jnp.where(hit, span_ids[None, :], 0), axis=1)
    slot_group = slot_span // CH_DEV
    slot_place = arrival[slot_span]
    q_for_slot = recv_q[(group_index - slot_group) % groups, slot_place]
    q_for_slot = q_for_slot.reshape(CAPC, SPAN, heads_local, HD)
    rows = lax.all_gather(neighbours, "tensor", axis=0, tiled=True)
    rows = rows.reshape(CAPC, KEYS, rows.shape[1])
    kv = jnp.einsum("skd,cde->cske", rows, kv_weight, preferred_element_type=jnp.float32)
    kv = kv.astype(jnp.bfloat16).reshape(2, CAPC, KEYS, heads_local, HD)
    keys, values = (kv[0], kv[1])
    attended = attend(q_for_slot, keys, values).reshape(CAPC, SPAN, cols)
    pick_a = (slot_group[None, None, :] == peer_ids) & (slot_place[None, None, :] == place_ids)
    send_a_idx = jnp.sum(
        jnp.where(pick_a, jnp.arange(CAPC, dtype=jnp.int32)[None, None, :], 0), axis=-1
    )
    send_a = attended[send_a_idx]
    by_shift = [send_a[group_index]]
    for k in range(1, groups):
        block = lax.dynamic_index_in_dim(send_a, (group_index + k) % groups, 0, keepdims=False)
        pairs = [(s, (s + k) % groups) for s in range(groups)]
        by_shift.append(lax.ppermute(block, ("section", "seq"), pairs))
    recv_a = jnp.stack(by_shift)
    shift_of = (group_index - own_owner) % groups
    attended_rows = recv_a[shift_of, own_arrival].reshape(tensor_size, -1, cols)
    partial = jnp.einsum(
        "srk,kn->srn", attended_rows, out_weight, preferred_element_type=jnp.float32
    ).astype(jnp.bfloat16)
    mixed = lax.psum_scatter(partial, "tensor", scatter_dimension=0, tiled=True)
    return mixed.reshape(-1, out_weight.shape[1])


def solution(mesh):
    placed = (
        P(("section", "seq"), "tensor"),
        P(("section", "seq", "tensor"), None),
        P(None, None, "tensor"),
        P("tensor", None),
        P(),
    )
    return jax.shard_map(
        on_device,
        mesh=mesh,
        in_specs=placed,
        out_specs=P(("section", "seq", "tensor"), None),
        check_vma=False,
    )
```

profile of v0, /device:TPU:0, one launch (start us, length us, event | category | flops | bytes accessed | tf_op | source)
XLA Modules:
  0.0 289.1 jit_solution(14220398571249133182)
XLA Ops:
  6.5 0.7 all-gather.2.cloned.1.call-update
  7.5 0.6 gather_fusion
  8.3 0.7 gather_fusion.1
  9.2 0.6 gather_fusion.3
  11.2 1.7 collective-permute-start
  12.9 2.7 collective-permute-start.1
  16.2 0.7 collective-permute-start.3
  17.5 0.9 collective-permute-done
  18.6 1.9 collective-permute-done.1
  20.7 0.7 collective-permute-done.2
  21.4 4.2 %collective-permute-done.4 = bf16[2,64,512]{2,1,0:T(8,128)(2,1)S(1)} collective-permute-done((bf16[2,64,512]{2,1,0:T(8,128)(2,1)S(1)}, bf16[2,64,512]{2,1,0:T(8,128)(2,1)S(1)}, u32[]{:S(2)}, u32[]{:S(2)}) %collective-permute-start.4) | collective-permute-done | bytes 131104 | tf_op jit(solution)/shard_map/ppermute | solution.py:57
  25.7 1.7 collective-permute-done.5
  28.1 116.7 %all-gather.2.cloned.1.call-done = bf16[1280,8192]{1,0:T(8,128)(2,1)} async-done(((bf16[80,8192]{1,0:T(8,128)(2,1)}), bf16[1280,8192]{1,0:T(8,128)(2,1)}) %all-gather.2.cloned.1.call-update) | async-done | bytes 20971536 | tf_op jit(solution)/shard_map/all_gather | solution.py:66
  144.8 26.7 %convert_bitcast_fusion = bf16[2,5,256,512]{2,3,1,0:T(8,128)(2,1)S(1)} fusion(bf16[5,256,8192,1]{2,1,0,3:T(8,128)(2,1)} %bitcast.146, bf16[2,8192,512]{2,1,0:T(8,128)(2,1)} %param.7), kind=kOutput, calls=%fused_computation.12 | convolution fusion | flops 21476147200 | bytes 40370176 | tf_op jit(solution)/shard_map/skd,cde->cske/dot_general | solution.py:68
  172.4 2.3 fusion.8
  175.6 1.5 collective-permute-start.7
  177.1 2.8 collective-permute-start.8
  180.3 0.8 collective-permute-start.10
  181.6 1.9 collective-permute-done.7
  183.6 0.9 collective-permute-done.8
  184.5 0.9 collective-permute-start.13
  185.8 5.7 %collective-permute-done.11 = bf16[2,64,512]{2,1,0:T(8,128)(2,1)S(1)} collective-permute-done((bf16[2,64,512]{2,1,0:T(8,128)(2,1)S(1)}, bf16[2,64,512]{2,1,0:T(8,128)(2,1)S(1)}, u32[]{:S(2)}, u32[]{:S(2)}) %collective-permute-start.11) | collective-permute-done | bytes 131104 | tf_op jit(solution)/shard_map/ppermute | solution.py:81
  192.2 8.7 %convolution_convert_fusion = bf16[16,20,8192]{2,1,0:T(8,128)(2,1)} fusion(bf16[16,20,512]{2,1,0:T(8,128)(2,1)S(1)} %reshape.368, bf16[512,8192]{1,0:T(8,128)(2,1)} %param.8), kind=kOutput, calls=%fused_computation.10 | convolution fusion | flops 2686976000 | bytes 13959168 | tf_op jit(solution)/shard_map/srk,kn->srn/dot_general | solution.py:85
  201.0 81.3 %reduce-scatter.4.cloned.1.call-done = bf16[1,20,8192]{2,1,0:T(8,128)(2,1)} async-done(((bf16[16,20,8192]{2,1,0:T(8,128)(2,1)}), bf16[1,20,8192]{2,1,0:T(8,128)(2,1)}) %reduce-scatter.4.cloned.1.call-update) | async-done | bytes 327696
  (72 shorter events, 8.1 us)
Async XLA Ops:
  6.5 3.9 %copy-start = (bf16[320,512]{1,0:T(8,128)(2,1)S(1)}, bf16[320,512]{1,0:T(8,128)(2,1)}, u32[]{:S(2)}) copy-start(bf16[320,512]{1,0:T(8,128)(2,1)} %param.5) | copy-start | bytes 983044
  6.5 0.9 copy-start.2
  6.5 138.2 %all-gather.2.cloned.1.call-start = ((), (), s32[]{:S(2)}) async-start(), calls=%async_computation.1 | async-start | bytes 22282240 | tf_op jit(solution)/shard_map/all_gather | solution.py:66
  7.3 275.0 %reduce-scatter.4.cloned.1.call-start = ((), (), s32[]{:S(2)}) async-start(), calls=%async_computation.2 | async-start | bytes 6684672
  11.2 7.2 %collective-permute-start = (bf16[2,64,512]{2,1,0:T(8,128)(2,1)S(1)}, bf16[2,64,512]{2,1,0:T(8,128)(2,1)S(1)}, u32[]{:S(2)}, u32[]{:S(2)}) collective-permute-start(bf16[2,64,512]{2,1,0:T(8,128)(2,1)S(1)} %get-tuple-element.21), channel_id=1, source_target_pairs={{0,16},{16,32},{32,48},{48,64},{64,80},{80,96},{96,112},{112,0},{1... | collective-permute-start | bytes 393224 | tf_op jit(solution)/shard_map/ppermute | solution.py:57
  12.9 7.6 %collective-permute-start.1 = (bf16[2,64,512]{2,1,0:T(8,128)(2,1)S(1)}, bf16[2,64,512]{2,1,0:T(8,128)(2,1)S(1)}, u32[]{:S(2)}, u32[]{:S(2)}) collective-permute-start(bf16[2,64,512]{2,1,0:T(8,128)(2,1)S(1)} %get-tuple-element.20), channel_id=1, source_target_pairs={{0,32},{16,48},{32,64},{48,80},{64,96},{80,112},{96,0},{112,16},{1... | collective-permute-start | bytes 393224 | tf_op jit(solution)/shard_map/ppermute | solution.py:57
  15.6 5.8 %collective-permute-start.2 = (bf16[2,64,512]{2,1,0:T(8,128)(2,1)S(1)}, bf16[2,64,512]{2,1,0:T(8,128)(2,1)S(1)}, u32[]{:S(2)}, u32[]{:S(2)}) collective-permute-start(bf16[2,64,512]{2,1,0:T(8,128)(2,1)S(1)} %get-tuple-element.19), channel_id=1, source_target_pairs={{0,48},{16,64},{32,80},{48,96},{64,112},{80,0},{96,16},{112,32},{1... | collective-permute-start | bytes 393224 | tf_op jit(solution)/shard_map/ppermute | solution.py:57
  16.2 5.2 %collective-permute-start.3 = (bf16[2,64,512]{2,1,0:T(8,128)(2,1)S(1)}, bf16[2,64,512]{2,1,0:T(8,128)(2,1)S(1)}, u32[]{:S(2)}, u32[]{:S(2)}) collective-permute-start(bf16[2,64,512]{2,1,0:T(8,128)(2,1)S(1)} %get-tuple-element.18), channel_id=1, source_target_pairs={{0,64},{16,80},{32,96},{48,112},{64,0},{80,16},{96,32},{112,48},{1... | collective-permute-start | bytes 393224 | tf_op jit(solution)/shard_map/ppermute | solution.py:57
  16.9 8.8 %collective-permute-start.4 = (bf16[2,64,512]{2,1,0:T(8,128)(2,1)S(1)}, bf16[2,64,512]{2,1,0:T(8,128)(2,1)S(1)}, u32[]{:S(2)}, u32[]{:S(2)}) collective-permute-start(bf16[2,64,512]{2,1,0:T(8,128)(2,1)S(1)} %get-tuple-element.17), channel_id=1, source_target_pairs={{0,80},{16,96},{32,112},{48,0},{64,16},{80,32},{96,48},{112,64},{1... | collective-permute-start | bytes 393224 | tf_op jit(solution)/shard_map/ppermute | solution.py:57
  18.4 8.9 %collective-permute-start.5 = (bf16[2,64,512]{2,1,0:T(8,128)(2,1)S(1)}, bf16[2,64,512]{2,1,0:T(8,128)(2,1)S(1)}, u32[]{:S(2)}, u32[]{:S(2)}) collective-permute-start(bf16[2,64,512]{2,1,0:T(8,128)(2,1)S(1)} %get-tuple-element.16), channel_id=1, source_target_pairs={{0,96},{16,112},{32,0},{48,16},{64,32},{80,48},{96,64},{112,80},{1... | collective-permute-start | bytes 393224 | tf_op jit(solution)/shard_map/ppermute | solution.py:57
  20.5 7.1 %collective-permute-start.6 = (bf16[2,64,512]{2,1,0:T(8,128)(2,1)S(1)}, bf16[2,64,512]{2,1,0:T(8,128)(2,1)S(1)}, u32[]{:S(2)}, u32[]{:S(2)}) collective-permute-start(bf16[2,64,512]{2,1,0:T(8,128)(2,1)S(1)} %get-tuple-element.15), channel_id=1, source_target_pairs={{0,112},{16,0},{32,16},{48,32},{64,48},{80,64},{96,80},{112,96},{1... | collective-permute-start | bytes 393224 | tf_op jit(solution)/shard_map/ppermute | solution.py:57
  175.6 8.0 %collective-permute-start.7 = (bf16[2,64,512]{2,1,0:T(8,128)(2,1)S(1)}, bf16[2,64,512]{2,1,0:T(8,128)(2,1)S(1)}, u32[]{:S(2)}, u32[]{:S(2)}) collective-permute-start(bf16[2,64,512]{2,1,0:T(8,128)(2,1)S(1)} %get-tuple-element.13), channel_id=1, source_target_pairs={{0,16},{16,32},{32,48},{48,64},{64,80},{80,96},{96,112},{112,0},{1... | collective-permute-start | bytes 393224 | tf_op jit(solution)/shard_map/ppermute | solution.py:81
  177.1 7.4 %collective-permute-start.8 = (bf16[2,64,512]{2,1,0:T(8,128)(2,1)S(1)}, bf16[2,64,512]{2,1,0:T(8,128)(2,1)S(1)}, u32[]{:S(2)}, u32[]{:S(2)}) collective-permute-start(bf16[2,64,512]{2,1,0:T(8,128)(2,1)S(1)} %get-tuple-element.12), channel_id=1, source_target_pairs={{0,32},{16,48},{32,64},{48,80},{64,96},{80,112},{96,0},{112,16},{1... | collective-permute-start | bytes 393224 | tf_op jit(solution)/shard_map/ppermute | solution.py:81
  179.9 5.9 %collective-permute-start.9 = (bf16[2,64,512]{2,1,0:T(8,128)(2,1)S(1)}, bf16[2,64,512]{2,1,0:T(8,128)(2,1)S(1)}, u32[]{:S(2)}, u32[]{:S(2)}) collective-permute-start(bf16[2,64,512]{2,1,0:T(8,128)(2,1)S(1)} %get-tuple-element.11), channel_id=1, source_target_pairs={{0,48},{16,64},{32,80},{48,96},{64,112},{80,0},{96,16},{112,32},{1... | collective-permute-start | bytes 393224 | tf_op jit(solution)/shard_map/ppermute | solution.py:81
  180.3 5.5 %collective-permute-start.10 = (bf16[2,64,512]{2,1,0:T(8,128)(2,1)S(1)}, bf16[2,64,512]{2,1,0:T(8,128)(2,1)S(1)}, u32[]{:S(2)}, u32[]{:S(2)}) collective-permute-start(bf16[2,64,512]{2,1,0:T(8,128)(2,1)S(1)} %get-tuple-element.10), channel_id=1, source_target_pairs={{0,64},{16,80},{32,96},{48,112},{64,0},{80,16},{96,32},{112,48},{1... | collective-permute-start | bytes 393224 | tf_op jit(solution)/shard_map/ppermute | solution.py:81
  181.2 10.3 %collective-permute-start.11 = (bf16[2,64,512]{2,1,0:T(8,128)(2,1)S(1)}, bf16[2,64,512]{2,1,0:T(8,128)(2,1)S(1)}, u32[]{:S(2)}, u32[]{:S(2)}) collective-permute-start(bf16[2,64,512]{2,1,0:T(8,128)(2,1)S(1)} %get-tuple-element.9), channel_id=1, source_target_pairs={{0,80},{16,96},{32,112},{48,0},{64,16},{80,32},{96,48},{112,64},{1... | collective-permute-start | bytes 393224 | tf_op jit(solution)/shard_map/ppermute | solution.py:81
  183.6 8.0 %collective-permute-start.12 = (bf16[2,64,512]{2,1,0:T(8,128)(2,1)S(1)}, bf16[2,64,512]{2,1,0:T(8,128)(2,1)S(1)}, u32[]{:S(2)}, u32[]{:S(2)}) collective-permute-start(bf16[2,64,512]{2,1,0:T(8,128)(2,1)S(1)} %get-tuple-element.8), channel_id=1, source_target_pairs={{0,96},{16,112},{32,0},{48,16},{64,32},{80,48},{96,64},{112,80},{1... | collective-permute-start | bytes 393224 | tf_op jit(solution)/shard_map/ppermute | solution.py:81
  184.5 7.1 %collective-permute-start.13 = (bf16[2,64,512]{2,1,0:T(8,128)(2,1)S(1)}, bf16[2,64,512]{2,1,0:T(8,128)(2,1)S(1)}, u32[]{:S(2)}, u32[]{:S(2)}) collective-permute-start(bf16[2,64,512]{2,1,0:T(8,128)(2,1)S(1)} %get-tuple-element.7), channel_id=1, source_target_pairs={{0,112},{16,0},{32,16},{48,32},{64,48},{80,64},{96,80},{112,96},{1... | collective-permute-start | bytes 393224 | tf_op jit(solution)/shard_map/ppermute | solution.py:81
  201.0 81.3 %copy-start.1 = (bf16[320,512]{1,0:T(8,128)(2,1)S(1)}, bf16[320,512]{1,0:T(8,128)(2,1)}, u32[]{:S(2)}) copy-start(bf16[320,512]{1,0:T(8,128)(2,1)} %param.5) | copy-start | bytes 983044
Sparse Core Ops, SparseCore 0:
  9.5 135.2 all-gather.1
  201.1 81.1 reduce-scatter.3
where the time goes:
time: 289 us
  waiting for transfers between devices  217 us (75%)
  matrix products  38 us (13%)
  between operations  13.8 us (5%)
  starting transfers between devices  13.5 us (5%)
  local copies, waits for them, and re-layouts  5.33 us (2%)
    all_gather x1, waiting for transfers between devices, on_device(): rows = lax.all_gather(neighbours, 'tensor', axis=0, tiled=True)  117 us
    unnamed x3, waiting for transfers between devices  82 us
    dot_general x1, matrix products, on_device(): jnp.einsum('skd,cde->cske', rows, kv_weight, preferred_element_type=jnp.f...  26.7 us
    ppermute x7, waiting for transfers between devices, on_device(): q_by_shift.append(lax.ppermute(block, ('section', 'seq'), pairs))  9.52 us
    ppermute x7, waiting for transfers between devices, on_device(): by_shift.append(lax.ppermute(block, ('section', 'seq'), pairs))  8.93 us
    dot_general x1, matrix products, on_device(): jnp.einsum('srk,kn->srn', attended_rows, out_weight, preferred_element_ty...  8.7 us
    ppermute x7, starting transfers between devices, on_device(): by_shift.append(lax.ppermute(block, ('section', 'seq'), pairs))  6.93 us
    ppermute x7, starting transfers between devices, on_device(): q_by_shift.append(lax.ppermute(block, ('section', 'seq'), pairs))  6.53 us
  transfers between devices with their start and end apart: 16, of which 12 were waited for; matrix products, arithmetic and copies ran while one was open for 2% of the time, Pallas kernels for 0%

commit v1 on v0

--- a/solution.py
+++ b/solution.py
@@ -63,7 +63,9 @@
     slot_place = arrival[slot_span]
     q_for_slot = recv_q[(group_index - slot_group) % groups, slot_place]
     q_for_slot = q_for_slot.reshape(CAPC, SPAN, heads_local, HD)
-    rows = lax.all_gather(neighbours, "tensor", axis=0, tiled=True)
+    rows = jnp.concatenate(
+        lax.all_to_all(jnp.stack([neighbours] * lax.axis_size("tensor")), "tensor", 0, 0), axis=0
+    )
     rows = rows.reshape(CAPC, KEYS, rows.shape[1])
     kv = jnp.einsum("skd,cde->cske", rows, kv_weight, preferred_element_type=jnp.float32)
     kv = kv.astype(jnp.bfloat16).reshape(2, CAPC, KEYS, heads_local, HD)

time: 289 us -> 479 us (1.66)
  waiting for transfers between devices: 217 us -> 390 us
  starting transfers between devices: 13.5 us -> 22.2 us
  local copies, waits for them, and re-layouts: 5.33 us -> 13.6 us
    all_to_all x0 -> x1, waiting for transfers between devices: none -> 292 us  [on_device(): lax.all_to_all(jnp.stack([neighbours] * lax.axis_size('tensor')), 'tensor...]
    all_gather x1 -> x0, waiting for transfers between devices: 117 us -> none  [on_device(): rows = lax.all_gather(neighbours, 'tensor', axis=0, tiled=True)]
    all_to_all x0 -> x1, starting transfers between devices: none -> 8.34 us  [on_device(): lax.all_to_all(jnp.stack([neighbours] * lax.axis_size('tensor')), 'tensor...]
    another operation x0 -> x1, local copies, waits for them, and re-layouts: none -> 8.29 us  [on_device(): jnp.stack([neighbours] * lax.axis_size('tensor'))]
    unnamed x3 -> x2, waiting for transfers between devices: 82 us -> 79.3 us
  transfers between devices with their start and end apart: 16 -> 16, of which waited for: 12 -> 12; matrix products, arithmetic and copies ran while one was open for 2% -> 1% of each run, Pallas kernels for 0% -> 0%
where the time goes in v1:
time: 479 us
  waiting for transfers between devices  390 us (81%)
  matrix products  38 us (8%)
  starting transfers between devices  22.2 us (5%)
  between operations  13.8 us (3%)
  local copies, waits for them, and re-layouts  13.6 us (3%)
    all_to_all x1, waiting for transfers between devices, on_device(): lax.all_to_all(jnp.stack([neighbours] * lax.axis_size('tensor')), 'tensor...  292 us
    unnamed x2, waiting for transfers between devices  79.3 us
    dot_general x1, matrix products, on_device(): jnp.einsum('skd,cde->cske', rows, kv_weight, preferred_element_type=jnp.f...  26.7 us
  transfers between devices with their start and end apart: 16, of which 12 were waited for; matrix products, arithmetic and copies ran while one was open for 1% of the time, Pallas kernels for 0%

profile of v1, /device:TPU:0, one launch (start us, length us, event | category | flops | bytes accessed | tf_op | source)
XLA Modules:
  0.0 478.6 jit_solution(17430976814937260755)
XLA Ops:
  6.5 8.3 %stack.67 = bf16[16,80,8192]{2,1,0:T(8,128)(2,1)} broadcast(bf16[80,8192]{1,0:T(8,128)(2,1)} %param.6), dimensions={1,2} | broadcast | bytes 22282240 | tf_op jit(solution)/shard_map/stack | solution.py:67
  14.8 8.3 %all-to-all-start = ((bf16[16,80,8192]{2,1,0:T(8,128)(2,1)}), bf16[16,80,8192]{2,1,0:T(8,128)(2,1)}, u32[]{:S(2)}, u32[]{:S(2)}) async-start(bf16[16,80,8192]{2,1,0:T(8,128)(2,1)} %stack.67), calls=%async_computation | async-start | bytes 41943040 | tf_op jit(solution)/shard_map/all_to_all | solution.py:67
  23.4 0.6 gather_fusion
  24.2 0.7 gather_fusion.1
  25.1 0.6 gather_fusion.3
  27.1 1.6 collective-permute-start
  28.6 2.7 collective-permute-start.1
  31.7 1.0 collective-permute-start.3
  33.3 1.6 collective-permute-done
  35.0 1.0 collective-permute-done.1
  35.9 0.8 collective-permute-start.6
  37.2 5.8 %collective-permute-done.4 = bf16[2,64,512]{2,1,0:T(8,128)(2,1)S(1)} collective-permute-done((bf16[2,64,512]{2,1,0:T(8,128)(2,1)S(1)}, bf16[2,64,512]{2,1,0:T(8,128)(2,1)S(1)}, u32[]{:S(2)}, u32[]{:S(2)}) %collective-permute-start.4) | collective-permute-done | bytes 131104 | tf_op jit(solution)/shard_map/ppermute | solution.py:57
  43.7 292.4 %all-to-all-done = bf16[16,80,8192]{2,1,0:T(8,128)(2,1)} async-done(((bf16[16,80,8192]{2,1,0:T(8,128)(2,1)}), bf16[16,80,8192]{2,1,0:T(8,128)(2,1)}, u32[]{:S(2)}, u32[]{:S(2)}) %all-to-all-start) | async-done | bytes 20971552 | tf_op jit(solution)/shard_map/all_to_all | solution.py:67
  336.1 26.7 %convert_bitcast_fusion = bf16[2,5,256,512]{2,3,1,0:T(8,128)(2,1)S(1)} fusion(bf16[5,256,8192,1]{2,1,0,3:T(8,128)(2,1)} %bitcast.2, bf16[2,8192,512]{2,1,0:T(8,128)(2,1)} %param.7), kind=kOutput, calls=%fused_computation.12 | convolution fusion | flops 21476147200 | bytes 40370176 | tf_op jit(solution)/shard_map/skd,cde->cske/dot_general | solution.py:70
  363.8 2.3 fusion.8
  366.9 1.6 collective-permute-start.7
  368.5 2.8 collective-permute-start.8
  371.3 1.3 collective-permute-start.10
  373.0 1.7 collective-permute-done.7
  374.7 1.1 collective-permute-done.8
  375.9 0.8 collective-permute-start.13
  377.1 5.7 %collective-permute-done.11 = bf16[2,64,512]{2,1,0:T(8,128)(2,1)S(1)} collective-permute-done((bf16[2,64,512]{2,1,0:T(8,128)(2,1)S(1)}, bf16[2,64,512]{2,1,0:T(8,128)(2,1)S(1)}, u32[]{:S(2)}, u32[]{:S(2)}) %collective-permute-start.11) | collective-permute-done | bytes 131104 | tf_op jit(solution)/shard_map/ppermute | solution.py:83
  383.7 8.7 %convolution_convert_fusion = bf16[16,20,8192]{2,1,0:T(8,128)(2,1)} fusion(bf16[16,20,512]{2,1,0:T(8,128)(2,1)S(1)} %reshape.366, bf16[512,8192]{1,0:T(8,128)(2,1)} %param.8), kind=kOutput, calls=%fused_computation.10 | convolution fusion | flops 2686976000 | bytes 13959168 | tf_op jit(solution)/shard_map/srk,kn->srn/dot_general | solution.py:87
  392.4 79.3 %reduce-scatter.4.cloned.1.call-done = bf16[1,20,8192]{2,1,0:T(8,128)(2,1)} async-done(((bf16[16,20,8192]{2,1,0:T(8,128)(2,1)}), bf16[1,20,8192]{2,1,0:T(8,128)(2,1)}) %reduce-scatter.4.cloned.1.call-update) | async-done | bytes 327696
  (72 shorter events, 7.4 us)
Async XLA Ops:
  6.5 19.8 %copy-start = (bf16[320,512]{1,0:T(8,128)(2,1)S(1)}, bf16[320,512]{1,0:T(8,128)(2,1)}, u32[]{:S(2)}) copy-start(bf16[320,512]{1,0:T(8,128)(2,1)} %param.5) | copy-start | bytes 983044
  14.8 8.5 %copy-start.2 = (s32[40]{0:T(128)S(1)}, s32[40]{0:T(128)}, u32[]{:S(2)}) copy-start(s32[40]{0:T(128)} %param.9) | copy-start | bytes 484
  14.8 321.3 %all-to-all-start = ((bf16[16,80,8192]{2,1,0:T(8,128)(2,1)}), bf16[16,80,8192]{2,1,0:T(8,128)(2,1)}, u32[]{:S(2)}, u32[]{:S(2)}) async-start(bf16[16,80,8192]{2,1,0:T(8,128)(2,1)} %stack.67), calls=%async_computation | async-start | bytes 41943040 | tf_op jit(solution)/shard_map/all_to_all | solution.py:67
  23.2 448.6 %reduce-scatter.4.cloned.1.call-start = ((), (), s32[]{:S(2)}) async-start(), calls=%async_computation.2 | async-start | bytes 6684672
  27.1 7.9 %collective-permute-start = (bf16[2,64,512]{2,1,0:T(8,128)(2,1)S(1)}, bf16[2,64,512]{2,1,0:T(8,128)(2,1)S(1)}, u32[]{:S(2)}, u32[]{:S(2)}) collective-permute-start(bf16[2,64,512]{2,1,0:T(8,128)(2,1)S(1)} %get-tuple-element.21), channel_id=1, source_target_pairs={{0,16},{16,32},{32,48},{48,64},{64,80},{80,96},{96,112},{112,0},{1... | collective-permute-start | bytes 393224 | tf_op jit(solution)/shard_map/ppermute | solution.py:57
  28.6 7.3 %collective-permute-start.1 = (bf16[2,64,512]{2,1,0:T(8,128)(2,1)S(1)}, bf16[2,64,512]{2,1,0:T(8,128)(2,1)S(1)}, u32[]{:S(2)}, u32[]{:S(2)}) collective-permute-start(bf16[2,64,512]{2,1,0:T(8,128)(2,1)S(1)} %get-tuple-element.20), channel_id=1, source_target_pairs={{0,32},{16,48},{32,64},{48,80},{64,96},{80,112},{96,0},{112,16},{1... | collective-permute-start | bytes 393224 | tf_op jit(solution)/shard_map/ppermute | solution.py:57
  31.4 5.8 %collective-permute-start.2 = (bf16[2,64,512]{2,1,0:T(8,128)(2,1)S(1)}, bf16[2,64,512]{2,1,0:T(8,128)(2,1)S(1)}, u32[]{:S(2)}, u32[]{:S(2)}) collective-permute-start(bf16[2,64,512]{2,1,0:T(8,128)(2,1)S(1)} %get-tuple-element.19), channel_id=1, source_target_pairs={{0,48},{16,64},{32,80},{48,96},{64,112},{80,0},{96,16},{112,32},{1... | collective-permute-start | bytes 393224 | tf_op jit(solution)/shard_map/ppermute | solution.py:57
  31.7 5.5 %collective-permute-start.3 = (bf16[2,64,512]{2,1,0:T(8,128)(2,1)S(1)}, bf16[2,64,512]{2,1,0:T(8,128)(2,1)S(1)}, u32[]{:S(2)}, u32[]{:S(2)}) collective-permute-start(bf16[2,64,512]{2,1,0:T(8,128)(2,1)S(1)} %get-tuple-element.18), channel_id=1, source_target_pairs={{0,64},{16,80},{32,96},{48,112},{64,0},{80,16},{96,32},{112,48},{1... | collective-permute-start | bytes 393224 | tf_op jit(solution)/shard_map/ppermute | solution.py:57
  32.6 10.3 %collective-permute-start.4 = (bf16[2,64,512]{2,1,0:T(8,128)(2,1)S(1)}, bf16[2,64,512]{2,1,0:T(8,128)(2,1)S(1)}, u32[]{:S(2)}, u32[]{:S(2)}) collective-permute-start(bf16[2,64,512]{2,1,0:T(8,128)(2,1)S(1)} %get-tuple-element.17), channel_id=1, source_target_pairs={{0,80},{16,96},{32,112},{48,0},{64,16},{80,32},{96,48},{112,64},{1... | collective-permute-start | bytes 393224 | tf_op jit(solution)/shard_map/ppermute | solution.py:57
  35.0 8.0 %collective-permute-start.5 = (bf16[2,64,512]{2,1,0:T(8,128)(2,1)S(1)}, bf16[2,64,512]{2,1,0:T(8,128)(2,1)S(1)}, u32[]{:S(2)}, u32[]{:S(2)}) collective-permute-start(bf16[2,64,512]{2,1,0:T(8,128)(2,1)S(1)} %get-tuple-element.16), channel_id=1, source_target_pairs={{0,96},{16,112},{32,0},{48,16},{64,32},{80,48},{96,64},{112,80},{1... | collective-permute-start | bytes 393224 | tf_op jit(solution)/shard_map/ppermute | solution.py:57
  35.9 7.2 %collective-permute-start.6 = (bf16[2,64,512]{2,1,0:T(8,128)(2,1)S(1)}, bf16[2,64,512]{2,1,0:T(8,128)(2,1)S(1)}, u32[]{:S(2)}, u32[]{:S(2)}) collective-permute-start(bf16[2,64,512]{2,1,0:T(8,128)(2,1)S(1)} %get-tuple-element.15), channel_id=1, source_target_pairs={{0,112},{16,0},{32,16},{48,32},{64,48},{80,64},{96,80},{112,96},{1... | collective-permute-start | bytes 393224 | tf_op jit(solution)/shard_map/ppermute | solution.py:57
  366.9 7.8 %collective-permute-start.7 = (bf16[2,64,512]{2,1,0:T(8,128)(2,1)S(1)}, bf16[2,64,512]{2,1,0:T(8,128)(2,1)S(1)}, u32[]{:S(2)}, u32[]{:S(2)}) collective-permute-start(bf16[2,64,512]{2,1,0:T(8,128)(2,1)S(1)} %get-tuple-element.13), channel_id=1, source_target_pairs={{0,16},{16,32},{32,48},{48,64},{64,80},{80,96},{96,112},{112,0},{1... | collective-permute-start | bytes 393224 | tf_op jit(solution)/shard_map/ppermute | solution.py:83
  368.5 7.4 %collective-permute-start.8 = (bf16[2,64,512]{2,1,0:T(8,128)(2,1)S(1)}, bf16[2,64,512]{2,1,0:T(8,128)(2,1)S(1)}, u32[]{:S(2)}, u32[]{:S(2)}) collective-permute-start(bf16[2,64,512]{2,1,0:T(8,128)(2,1)S(1)} %get-tuple-element.12), channel_id=1, source_target_pairs={{0,32},{16,48},{32,64},{48,80},{64,96},{80,112},{96,0},{112,16},{1... | collective-permute-start | bytes 393224 | tf_op jit(solution)/shard_map/ppermute | solution.py:83
  371.3 5.8 %collective-permute-start.9 = (bf16[2,64,512]{2,1,0:T(8,128)(2,1)S(1)}, bf16[2,64,512]{2,1,0:T(8,128)(2,1)S(1)}, u32[]{:S(2)}, u32[]{:S(2)}) collective-permute-start(bf16[2,64,512]{2,1,0:T(8,128)(2,1)S(1)} %get-tuple-element.11), channel_id=1, source_target_pairs={{0,48},{16,64},{32,80},{48,96},{64,112},{80,0},{96,16},{112,32},{1... | collective-permute-start | bytes 393224 | tf_op jit(solution)/shard_map/ppermute | solution.py:83
  371.3 5.8 %collective-permute-start.10 = (bf16[2,64,512]{2,1,0:T(8,128)(2,1)S(1)}, bf16[2,64,512]{2,1,0:T(8,128)(2,1)S(1)}, u32[]{:S(2)}, u32[]{:S(2)}) collective-permute-start(bf16[2,64,512]{2,1,0:T(8,128)(2,1)S(1)} %get-tuple-element.10), channel_id=1, source_target_pairs={{0,64},{16,80},{32,96},{48,112},{64,0},{80,16},{96,32},{112,48},{1... | collective-permute-start | bytes 393224 | tf_op jit(solution)/shard_map/ppermute | solution.py:83
  372.6 10.3 %collective-permute-start.11 = (bf16[2,64,512]{2,1,0:T(8,128)(2,1)S(1)}, bf16[2,64,512]{2,1,0:T(8,128)(2,1)S(1)}, u32[]{:S(2)}, u32[]{:S(2)}) collective-permute-start(bf16[2,64,512]{2,1,0:T(8,128)(2,1)S(1)} %get-tuple-element.9), channel_id=1, source_target_pairs={{0,80},{16,96},{32,112},{48,0},{64,16},{80,32},{96,48},{112,64},{1... | collective-permute-start | bytes 393224 | tf_op jit(solution)/shard_map/ppermute | solution.py:83
  374.7 8.1 %collective-permute-start.12 = (bf16[2,64,512]{2,1,0:T(8,128)(2,1)S(1)}, bf16[2,64,512]{2,1,0:T(8,128)(2,1)S(1)}, u32[]{:S(2)}, u32[]{:S(2)}) collective-permute-start(bf16[2,64,512]{2,1,0:T(8,128)(2,1)S(1)} %get-tuple-element.8), channel_id=1, source_target_pairs={{0,96},{16,112},{32,0},{48,16},{64,32},{80,48},{96,64},{112,80},{1... | collective-permute-start | bytes 393224 | tf_op jit(solution)/shard_map/ppermute | solution.py:83
  375.9 7.2 %collective-permute-start.13 = (bf16[2,64,512]{2,1,0:T(8,128)(2,1)S(1)}, bf16[2,64,512]{2,1,0:T(8,128)(2,1)S(1)}, u32[]{:S(2)}, u32[]{:S(2)}) collective-permute-start(bf16[2,64,512]{2,1,0:T(8,128)(2,1)S(1)} %get-tuple-element.7), channel_id=1, source_target_pairs={{0,112},{16,0},{32,16},{48,32},{64,48},{80,64},{96,80},{112,96},{1... | collective-permute-start | bytes 393224 | tf_op jit(solution)/shard_map/ppermute | solution.py:83
  392.4 79.3 %copy-start.1 = (bf16[320,512]{1,0:T(8,128)(2,1)S(1)}, bf16[320,512]{1,0:T(8,128)(2,1)}, u32[]{:S(2)}) copy-start(bf16[320,512]{1,0:T(8,128)(2,1)} %param.5) | copy-start | bytes 983044
Sparse Core Ops, SparseCore 0:
  392.6 79.1 reduce-scatter.3
